TPU v7x, 512 devices: a whole 4x8x8 slice. The times are simulated.
512 devices in a mesh: ctx: 256 (over z, y, x_lo, core), kvh: 2 (over x_hi).
Axes of the slice: x: 4 (x_hi: 2, x_lo: 2; x = x_hi * 2 + x_lo), y: 8, z: 8, core: 2. Of those that a mesh axis runs over, the one named last changes fastest.
Arguments:
- queries: bfloat16 [65536, 64, 128], P('ctx', 'kvh'), may hold values from -110 to 110
- key_value: bfloat16 [2, 65536, 8, 128], P(None, 'ctx', 'kvh'), may hold values from -5 to 5
- span_table: int32 [512], replicated, may hold values from 0 to 511, as said below
Outputs:
- attended: bfloat16 [65536, 8192], P(('ctx', 'kvh'))
Inputs may be any that keep to these rules, and one draw needn't show every extreme that they name: `span_table`: entries 2 d and 2 d + 1 are the spans of ctx index d: the first below 256, the second 256 or above; every span of 0 to 511 appears exactly once.
All inputs are finite; a program needn't handle non-finite values.
Results may differ from a plain program's by a relative error of at most 0.0065.
Values may be sent and summed in bfloat16 or wider, within the bound.
No kernel may reach another device: no remote copies, remote signals or barrier semaphores. Data moves between devices by JAX's collectives and lax.ppermute only.
A program may use at most 64 MiB of HBM per device.

v0:
```python
import jax
import jax.numpy as jnp
from jax import lax
from jax.sharding import PartitionSpec as P

STEPS = 4


def passed_along(value, axis, steps):
    count = lax.axis_size(axis)
    pairs = [(source, (source + steps) % count) for source in range(count)]
    return lax.ppermute(value, axis, pairs)


def body(queries, key_value, span_table):
    rows = queries.shape[0]
    heads_here = queries.shape[1]
    head_size = queries.shape[2]
    kv_here = key_value.shape[2]
    group = heads_here // kv_here
    span = rows // 2
    scale = 1.0 / head_size**0.5
    cycle = lax.axis_size("ctx")
    myself = lax.axis_index("ctx")
    table = span_table.reshape(cycle, 2)
    offsets = jnp.arange(span, dtype=jnp.int32)

    def positions_of(device):
        pair = lax.dynamic_index_in_dim(table, device, 0, keepdims=False)
        return (pair[:, None] * span + offsets[None, :]).reshape(rows)

    query_pos = positions_of(myself)
    grouped = queries.reshape(rows, kv_here, group, head_size)

    def attend(carry, block, source):
        run_max, numer, denom = carry
        key_pos = positions_of(source)
        scores = (
            jnp.einsum("qghd,kgd->ghqk", grouped, block[0], preferred_element_type=jnp.float32)
            * scale
        )
        visible = (key_pos[None, :] <= query_pos[:, None])[None, None]
        masked = jnp.where(visible, scores, -jnp.inf)
        block_max = jnp.maximum(jnp.max(masked, axis=-1), jnp.float32(-1e30))
        weight = jnp.exp(masked - block_max[..., None])
        block_sum = jnp.sum(weight, axis=-1)
        block_out = jnp.einsum(
            "ghqk,kgd->ghqd",
            weight.astype(jnp.bfloat16),
            block[1],
            preferred_element_type=jnp.float32,
        )
        new_max = jnp.maximum(run_max, block_max)
        old_factor = jnp.exp(run_max - new_max)
        new_factor = jnp.exp(block_max - new_max)
        numer = numer * old_factor[..., None] + block_out * new_factor[..., None]
        denom = denom * old_factor + block_sum * new_factor
        return (new_max, numer, denom)

    start = (
        jnp.full((kv_here, group, rows), -1e30, jnp.float32),
        jnp.zeros((kv_here, group, rows, head_size), jnp.float32),
        jnp.zeros((kv_here, group, rows), jnp.float32),
    )
    carry = attend(start, key_value, myself)
    moving = key_value
    for distance in range(1, STEPS):
        moving = passed_along(moving, "ctx", 1)
        carry = attend(carry, moving, (myself - distance) % cycle)
    run_max, numer, denom = carry
    result = numer / denom[..., None]
    local_out = (
        jnp.transpose(result, (2, 0, 1, 3))
        .reshape(rows, heads_here * head_size)
        .astype(jnp.bfloat16)
    )
    return lax.all_to_all(local_out, "kvh", split_axis=0, concat_axis=1, tiled=True)


def solution(mesh):
    in_specs = (P("ctx", "kvh", None), P(None, "ctx", "kvh", None), P())
    out_specs = P(("ctx", "kvh"), None)
    return jax.shard_map(body, mesh=mesh, in_specs=in_specs, out_specs=out_specs, check_vma=False)
```

profile of v0, /device:TPU:4, one launch (start us, length us, event | category | flops | bytes accessed | tf_op | source)
XLA Modules:
  0.0 106.6 jit_solution(826526950033051445)
XLA Ops:
  0.0 0.0 copy-start
  0.0 1.3 %copy.27 = bf16[2,256,4,128]{3,1,2,0:T(8,128)(2,1)S(1)} copy(bf16[2,256,4,128]{3,2,1,0:T(4,128)(2,1)} %param.4) | data formatting | bytes 1048576 | tf_op args[1]
  1.3 1.9 %collective-permute-start = (bf16[2,256,4,128]{3,1,2,0:T(8,128)(2,1)S(1)}, bf16[2,256,4,128]{3,1,2,0:T(8,128)(2,1)S(1)}, u32[]{:S(2)}, u32[]{:S(2)}) collective-permute-start(bf16[2,256,4,128]{3,1,2,0:T(8,128)(2,1)S(1)} %copy.27), channel_id=1, source_target_pairs={{0,2},{2,4},{4,6},{6,8},{8,10},{10,12},{12,14},{14,16},{16,18},{18... | collective-permute-start | bytes 1572872 | tf_op jit(solution)/shard_map/ppermute | solution.py:12
  3.3 0.8 reshape.328
  4.1 0.1 add_bitcast_fusion
  4.2 0.1 add_bitcast_fusion.2
  4.3 0.2 broadcast_compare_fusion
  4.5 0.0 copy-done
  4.5 2.1 %fusion.8 = (f32[4,8,256]{2,1,0:T(8,128)S(1)}, f32[4,256,256,8]{2,1,3,0:T(8,128)S(1)}) fusion(pred[256,256]{0,1:T(8,128)(4,1)S(1)} %get-tuple-element.23, bf16[256,4,8,128]{3,2,1,0:T(8,128)(2,1)S(1)} %bitcast.239, bf16[2,256,4,128]{3,1,2,0:T(8,128)(2,1)S(1)} %copy.27), kind=kOutput, calls=%fused_computation.16 | convolution fusion | flops 543154176 | bytes 10846208 | tf_op jit(solution)/shard_map/qghd,kgd->ghqk/dot_general | solution.py:39
  6.7 2.4 %fusion.18 = f32[4,8,256,128]{3,2,1,0:T(8,128)S(1)} fusion(f32[4,256,256,8]{2,1,3,0:T(8,128)S(1)} %get-tuple-element.30, f32[4,8,256]{2,1,0:T(8,128)S(1)} %broadcast_maximum_fusion.3, pred[256,256]{0,1:T(8,128)(4,1)S(1)} %get-tuple-element.23, bf16[2,256,4,128]{3,1,2,0:T(8,128)(2,1)S(1)} %copy.27), kind=kOutput, calls=%fused_computation.23 | convolution fusion | flops 545259520 | bytes 12943360 | tf_op jit(solution)/shard_map/ghqk,kgd->ghqd/dot_general | solution.py:47
  9.0 1.8 %fusion = f32[4,8,256]{2,1,0:T(8,128)S(1)} fusion(f32[4,256,256,8]{2,1,3,0:T(8,128)S(1)} %get-tuple-element.30, f32[4,8,256]{2,1,0:T(8,128)S(1)} %broadcast_maximum_fusion.3, pred[256,256]{0,1:T(8,128)(4,1)S(1)} %get-tuple-element.23), kind=kLoop, calls=%fused_computation.8 | loop fusion | flops 8380416 | bytes 8519680 | tf_op jit(solution)/shard_map/reduce_sum | solution.py:46
  10.8 11.2 %collective-permute-done = bf16[2,256,4,128]{3,1,2,0:T(8,128)(2,1)S(1)} collective-permute-done((bf16[2,256,4,128]{3,1,2,0:T(8,128)(2,1)S(1)}, bf16[2,256,4,128]{3,1,2,0:T(8,128)(2,1)S(1)}, u32[]{:S(2)}, u32[]{:S(2)}) %collective-permute-start) | collective-permute-done | bytes 524320 | tf_op jit(solution)/shard_map/ppermute | solution.py:12
  22.1 2.1 %fusion.9 = (f32[4,8,256]{2,1,0:T(8,128)S(1)}, f32[4,256,256,8]{2,1,3,0:T(8,128)S(1)}) fusion(pred[256,256]{0,1:T(8,128)(4,1)S(1)} %get-tuple-element.24, bf16[256,4,8,128]{3,2,1,0:T(8,128)(2,1)S(1)} %bitcast.242, bf16[2,256,4,128]{3,1,2,0:T(8,128)(2,1)S(1)} %collective-permute-done), kind=kOutput, calls=%fused_computation.17 | convolution fusion | flops 543154176 | bytes 10846208 | tf_op jit(solution)/shard_map/qghd,kgd->ghqk/dot_general | solution.py:39
  24.2 2.1 %collective-permute-start.1 = (bf16[2,256,4,128]{3,1,2,0:T(8,128)(2,1)S(1)}, bf16[2,256,4,128]{3,1,2,0:T(8,128)(2,1)S(1)}, u32[]{:S(2)}, u32[]{:S(2)}) collective-permute-start(bf16[2,256,4,128]{3,1,2,0:T(8,128)(2,1)S(1)} %collective-permute-done), channel_id=1, source_target_pairs={{0,2},{2,4},{4,6},{6,8},{8,10},{10,12},{12,14},{14,16},{16,18},{18... | collective-permute-start | bytes 1572872 | tf_op jit(solution)/shard_map/ppermute | solution.py:12
  26.3 2.4 %fusion.16 = f32[4,8,256,128]{3,2,1,0:T(8,128)S(1)} fusion(f32[4,256,256,8]{2,1,3,0:T(8,128)S(1)} %get-tuple-element.28, f32[4,8,256]{2,1,0:T(8,128)S(1)} %broadcast_maximum_fusion.2, pred[256,256]{0,1:T(8,128)(4,1)S(1)} %get-tuple-element.24, bf16[2,256,4,128]{3,1,2,0:T(8,128)(2,1)S(1)} %collective-permute-done), kind=kOutput, calls=%fused_computation.22 | convolution fusion | flops 545259520 | bytes 12943360 | tf_op jit(solution)/shard_map/ghqk,kgd->ghqd/dot_general | solution.py:47
  28.7 1.8 %fusion.2 = f32[4,8,256]{2,1,0:T(8,128)S(1)} fusion(f32[4,256,256,8]{2,1,3,0:T(8,128)S(1)} %get-tuple-element.28, f32[4,8,256]{2,1,0:T(8,128)S(1)} %broadcast_maximum_fusion.2, pred[256,256]{0,1:T(8,128)(4,1)S(1)} %get-tuple-element.24), kind=kLoop, calls=%fused_computation.10 | loop fusion | flops 8380416 | bytes 8519680 | tf_op jit(solution)/shard_map/reduce_sum | solution.py:46
  30.5 8.4 %collective-permute-done.1 = bf16[2,256,4,128]{3,1,2,0:T(8,128)(2,1)S(1)} collective-permute-done((bf16[2,256,4,128]{3,1,2,0:T(8,128)(2,1)S(1)}, bf16[2,256,4,128]{3,1,2,0:T(8,128)(2,1)S(1)}, u32[]{:S(2)}, u32[]{:S(2)}) %collective-permute-start.1) | collective-permute-done | bytes 524320 | tf_op jit(solution)/shard_map/ppermute | solution.py:12
  38.9 2.1 %fusion.10 = (f32[4,8,256]{2,1,0:T(8,128)S(1)}, f32[4,256,256,8]{2,1,3,0:T(8,128)S(1)}) fusion(pred[256,256]{0,1:T(8,128)(4,1)S(1)} %get-tuple-element.22, bf16[256,4,8,128]{3,2,1,0:T(8,128)(2,1)S(1)} %bitcast.241, bf16[2,256,4,128]{3,1,2,0:T(8,128)(2,1)S(1)} %collective-permute-done.1), kind=kOutput, calls=%fused_computation.18 | convolution fusion | flops 543154176 | bytes 10846208 | tf_op jit(solution)/shard_map/qghd,kgd->ghqk/dot_general | solution.py:39
  41.1 2.1 %collective-permute-start.2 = (bf16[2,256,4,128]{3,1,2,0:T(8,128)(2,1)S(1)}, bf16[2,256,4,128]{3,1,2,0:T(8,128)(2,1)S(1)}, u32[]{:S(2)}, u32[]{:S(2)}) collective-permute-start(bf16[2,256,4,128]{3,1,2,0:T(8,128)(2,1)S(1)} %collective-permute-done.1), channel_id=1, source_target_pairs={{0,2},{2,4},{4,6},{6,8},{8,10},{10,12},{12,14},{14,16},{16,18},{18... | collective-permute-start | bytes 1572872 | tf_op jit(solution)/shard_map/ppermute | solution.py:12
  43.3 2.4 %fusion.14 = f32[4,8,256,128]{3,2,1,0:T(8,128)S(1)} fusion(f32[4,256,256,8]{2,1,3,0:T(8,128)S(1)} %get-tuple-element.26, f32[4,8,256]{2,1,0:T(8,128)S(1)} %broadcast_maximum_fusion.1, pred[256,256]{0,1:T(8,128)(4,1)S(1)} %get-tuple-element.22, bf16[2,256,4,128]{3,1,2,0:T(8,128)(2,1)S(1)} %collective-permute-done.1), kind=kOutput, calls=%fused_computation.21 | convolution fusion | flops 545259520 | bytes 12943360 | tf_op jit(solution)/shard_map/ghqk,kgd->ghqd/dot_general | solution.py:47
  45.6 1.8 %fusion.4 = f32[4,8,256]{2,1,0:T(8,128)S(1)} fusion(f32[4,256,256,8]{2,1,3,0:T(8,128)S(1)} %get-tuple-element.26, f32[4,8,256]{2,1,0:T(8,128)S(1)} %broadcast_maximum_fusion.1, pred[256,256]{0,1:T(8,128)(4,1)S(1)} %get-tuple-element.22), kind=kLoop, calls=%fused_computation.12 | loop fusion | flops 8380416 | bytes 8519680 | tf_op jit(solution)/shard_map/reduce_sum | solution.py:46
  47.4 8.4 %collective-permute-done.2 = bf16[2,256,4,128]{3,1,2,0:T(8,128)(2,1)S(1)} collective-permute-done((bf16[2,256,4,128]{3,1,2,0:T(8,128)(2,1)S(1)}, bf16[2,256,4,128]{3,1,2,0:T(8,128)(2,1)S(1)}, u32[]{:S(2)}, u32[]{:S(2)}) %collective-permute-start.2) | collective-permute-done | bytes 524320 | tf_op jit(solution)/shard_map/ppermute | solution.py:12
  55.8 2.1 %fusion.11 = (f32[4,8,256]{2,1,0:T(8,128)S(1)}, f32[4,256,256,8]{2,1,3,0:T(8,128)S(1)}) fusion(pred[256,256]{0,1:T(8,128)(4,1)S(1)} %get-tuple-element.21, bf16[256,4,8,128]{3,2,1,0:T(8,128)(2,1)S(1)} %bitcast.240, bf16[2,256,4,128]{3,1,2,0:T(8,128)(2,1)S(1)} %collective-permute-done.2), kind=kOutput, calls=%fused_computation.19 | convolution fusion | flops 543154176 | bytes 10846208 | tf_op jit(solution)/shard_map/qghd,kgd->ghqk/dot_general | solution.py:39
  58.0 1.8 %fusion.6 = f32[4,8,256]{2,1,0:T(8,128)S(1)} fusion(f32[4,256,256,8]{2,1,3,0:T(8,128)S(1)} %get-tuple-element.32, f32[4,8,256]{2,1,0:T(8,128)S(1)} %broadcast_maximum_fusion, pred[256,256]{0,1:T(8,128)(4,1)S(1)} %get-tuple-element.21), kind=kLoop, calls=%fused_computation.14 | loop fusion | flops 8380416 | bytes 8519680 | tf_op jit(solution)/shard_map/reduce_sum | solution.py:46
  59.8 0.1 fusion.57
  59.8 12.3 %fusion.22 = bf16[256,4,8,128]{3,0,2,1:T(8,128)(2,1)S(1)} fusion(f32[4,8,256,128]{3,2,1,0:T(8,128)S(1)} %fusion.14, f32[4,8,256,128]{3,2,1,0:T(8,128)S(1)} %fusion.16, f32[4,8,256,128]{3,2,1,0:T(8,128)S(1)} %fusion.18, f32[256,4,8]{0,2,1:T(8,128)S(1)} %get-tuple-element.7, f32[256,4,8]{0,2,1:T(8,128)S(1)} %get-tuple-element.10, ...), kind=kOutput, calls=%fused_computation.27 | convolution fusion | flops 558891008 | bytes 23724032 | tf_op jit(solution)/shard_map/ghqk,kgd->ghqd/dot_general | solution.py:47
  72.1 2.7 %copy.38 = bf16[256,4,8,128]{3,2,1,0:T(8,128)(2,1)} copy(bf16[256,4,8,128]{3,0,2,1:T(8,128)(2,1)S(1)} %fusion.22) | data formatting | bytes 4194304 | tf_op jit(solution)/shard_map/convert_element_type | solution.py:75
  74.8 4.2 %convert_element_type.24 = bf16[2,128,4096]{2,1,0:T(8,128)(2,1)} reshape(bf16[256,4,8,128]{3,2,1,0:T(8,128)(2,1)} %copy.38) | data formatting | bytes 4194304 | tf_op jit(solution)/shard_map/convert_element_type | solution.py:75
  79.0 19.5 %all_to_all.16 = bf16[2,128,4096]{2,1,0:T(8,128)(2,1)} all-to-all(bf16[2,128,4096]{2,1,0:T(8,128)(2,1)} %convert_element_type.24), channel_id=1, replica_groups=mesh['ctx'=256,'kvh'=2] {'kvh'}, dimensions={0} | all-to-all | bytes 4194304 | tf_op jit(solution)/shard_map/all_to_all | solution.py:77
  98.4 4.1 %copy.39 = bf16[128,2,4096]{0,2,1:T(8,128)(2,1)} copy(bf16[128,2,4096]{2,0,1:T(8,128)(2,1)} %bitcast.243) | data formatting | bytes 4194304 | tf_op jit(solution)/shard_map/all_to_all | solution.py:77
  102.5 4.1 %copy.40 = bf16[128,8192]{1,0:T(8,128)(2,1)} copy(bf16[128,8192]{0,1:T(8,128)(2,1)} %bitcast.244) | data formatting | bytes 4194304 | tf_op jit(solution)/shard_map/all_to_all | solution.py:77
  (6 shorter events, 0.1 us)
Async XLA Ops:
  0.0 4.5 %copy-start = (bf16[256,32,128]{2,1,0:T(8,128)(2,1)S(1)}, bf16[256,32,128]{2,1,0:T(8,128)(2,1)}, u32[]{:S(2)}) copy-start(bf16[256,32,128]{2,1,0:T(8,128)(2,1)} %param.3) | copy-start | bytes 6291460
  1.3 20.8 %collective-permute-start = (bf16[2,256,4,128]{3,1,2,0:T(8,128)(2,1)S(1)}, bf16[2,256,4,128]{3,1,2,0:T(8,128)(2,1)S(1)}, u32[]{:S(2)}, u32[]{:S(2)}) collective-permute-start(bf16[2,256,4,128]{3,1,2,0:T(8,128)(2,1)S(1)} %copy.27), channel_id=1, source_target_pairs={{0,2},{2,4},{4,6},{6,8},{8,10},{10,12},{12,14},{14,16},{16,18},{18... | collective-permute-start | bytes 1572872 | tf_op jit(solution)/shard_map/ppermute | solution.py:12
  24.2 14.7 %collective-permute-start.1 = (bf16[2,256,4,128]{3,1,2,0:T(8,128)(2,1)S(1)}, bf16[2,256,4,128]{3,1,2,0:T(8,128)(2,1)S(1)}, u32[]{:S(2)}, u32[]{:S(2)}) collective-permute-start(bf16[2,256,4,128]{3,1,2,0:T(8,128)(2,1)S(1)} %collective-permute-done), channel_id=1, source_target_pairs={{0,2},{2,4},{4,6},{6,8},{8,10},{10,12},{12,14},{14,16},{16,18},{18... | collective-permute-start | bytes 1572872 | tf_op jit(solution)/shard_map/ppermute | solution.py:12
  41.1 14.7 %collective-permute-start.2 = (bf16[2,256,4,128]{3,1,2,0:T(8,128)(2,1)S(1)}, bf16[2,256,4,128]{3,1,2,0:T(8,128)(2,1)S(1)}, u32[]{:S(2)}, u32[]{:S(2)}) collective-permute-start(bf16[2,256,4,128]{3,1,2,0:T(8,128)(2,1)S(1)} %collective-permute-done.1), channel_id=1, source_target_pairs={{0,2},{2,4},{4,6},{6,8},{8,10},{10,12},{12,14},{14,16},{16,18},{18... | collective-permute-start | bytes 1572872 | tf_op jit(solution)/shard_map/ppermute | solution.py:12
where the time goes:
time: 107 us
  waiting for transfers between devices  28.1 us (26%)
  matrix products  27.9 us (26%)
  blocking collectives  19.5 us (18%)
  local copies, waits for them, and re-layouts  17.1 us (16%)
  other arithmetic  7.65 us (7%)
  starting transfers between devices  6.16 us (6%)
    ppermute x3, waiting for transfers between devices, passed_along(): return lax.ppermute(value, axis, pairs)  28.1 us
    all_to_all x1, blocking collectives, body(): lax.all_to_all(local_out, 'kvh', split_axis=0, concat_axis=1, tiled=True)  19.5 us
    dot_general x4, matrix products, attend(): jnp.einsum('ghqk,kgd->ghqd', weight.astype(jnp.bfloat16), block[1], prefe...  19.3 us
    dot_general x4, matrix products, attend(): jnp.einsum('qghd,kgd->ghqk', grouped, block[0], preferred_element_type=jn...  8.5 us
    all_to_all x2, local copies, waits for them, and re-layouts, body(): lax.all_to_all(local_out, 'kvh', split_axis=0, concat_axis=1, tiled=True)  8.14 us
    reduce_sum x4, other arithmetic, attend(): block_sum = jnp.sum(weight, axis=-1)  7.15 us
    convert_element_type x2, local copies, waits for them, and re-layouts, body(): local_out = jnp.transpose(result, (2, 0, 1, 3)).reshape(rows, heads_here...  6.85 us
    ppermute x3, starting transfers between devices, passed_along(): return lax.ppermute(value, axis, pairs)  6.16 us
  transfers between devices with their start and end apart: 3, of which 3 were waited for; matrix products, arithmetic and copies ran while one was open for 15% of the time, Pallas kernels for 0%

commit v1 on v0

--- a/solution.py
+++ b/solution.py
@@ -74,7 +74,16 @@
         .reshape(rows, heads_here * head_size)
         .astype(jnp.bfloat16)
     )
-    return lax.all_to_all(local_out, "kvh", split_axis=0, concat_axis=1, tiled=True)
+    produce_series_all = lambda x_local: jnp.concatenate(
+        lax.all_to_all(
+            jnp.stack(jnp.split(x_local, lax.axis_size("kvh"), 0), 0),
+            axis_name="kvh",
+            split_axis=0,
+            concat_axis=0,
+        ),
+        1,
+    )
+    return produce_series_all(local_out)
 
 
 def solution(mesh):

time: 107 us -> 90.2 us (0.84)
  local copies, waits for them, and re-layouts: 17.1 us -> 9.04 us
  matrix products: 27.9 us -> 21.7 us
  blocking collectives: 19.5 us -> 17.7 us
  waiting for transfers between devices: 28.1 us -> 27 us
    all_to_all x2 -> x0, local copies, waits for them, and re-layouts: 8.14 us -> none  [body(): lax.all_to_all(local_out, 'kvh', split_axis=0, concat_axis=1, tiled=True)]
    dot_general x4, matrix products: 19.3 us -> 12.3 us  [attend(): jnp.einsum('ghqk,kgd->ghqd', weight.astype(jnp.bfloat16), block[1], prefe...]
    convert_element_type x2 -> x0, local copies, waits for them, and re-layouts: 6.85 us -> none  [body(): local_out = jnp.transpose(result, (2, 0, 1, 3)).reshape(rows, heads_here...]
    reshape x0 -> x1, local copies, waits for them, and re-layouts: none -> 4.07 us  [body(): jnp.concatenate(lax.all_to_all(jnp.stack(jnp.split(x_local, lax.axis_size...]
    all_to_all x1, blocking collectives: 19.5 us -> 17.7 us  [body(): lax.all_to_all(jnp.stack(jnp.split(x_local, lax.axis_size('kvh'), 0), 0),...]
    split x0 -> x1, local copies, waits for them, and re-layouts: none -> 1.68 us  [body(): jnp.split(x_local, lax.axis_size('kvh'), 0)]
    ppermute x3, waiting for transfers between devices: 28.1 us -> 27 us  [passed_along(): return lax.ppermute(value, axis, pairs)]
  transfers between devices with their start and end apart: 3 -> 3, of which waited for: 3 -> 3; matrix products, arithmetic and copies ran while one was open for 15% -> 19% of each run, Pallas kernels for 0% -> 0%
where the time goes in v1:
time: 90.2 us; the launch traced here: 89.8 us
  waiting for transfers between devices  27 us (30%)
  matrix products  21.7 us (24%)
  blocking collectives  17.7 us (20%)
  local copies, waits for them, and re-layouts  9.04 us (10%)
  other arithmetic  7.87 us (9%)
  starting transfers between devices  6.16 us (7%)
    ppermute x3, waiting for transfers between devices, passed_along(): return lax.ppermute(value, axis, pairs)  27 us
    all_to_all x1, blocking collectives, body(): lax.all_to_all(jnp.stack(jnp.split(x_local, lax.axis_size('kvh'), 0), 0),...  17.7 us
    dot_general x4, matrix products, attend(): jnp.einsum('ghqk,kgd->ghqd', weight.astype(jnp.bfloat16), block[1], prefe...  12.3 us
    dot_general x4, matrix products, attend(): jnp.einsum('qghd,kgd->ghqk', grouped, block[0], preferred_element_type=jn...  9.49 us
    reduce_sum x4, other arithmetic, attend(): block_sum = jnp.sum(weight, axis=-1)  7.19 us
    ppermute x3, starting transfers between devices, passed_along(): return lax.ppermute(value, axis, pairs)  6.16 us
    reshape x1, local copies, waits for them, and re-layouts, body(): jnp.concatenate(lax.all_to_all(jnp.stack(jnp.split(x_local, lax.axis_size...  4.07 us
  transfers between devices with their start and end apart: 3, of which 3 were waited for; matrix products, arithmetic and copies ran while one was open for 19% of the time, Pallas kernels for 0%

profile of v1, /device:TPU:4, one launch (start us, length us, event | category | flops | bytes accessed | tf_op | source)
XLA Modules:
  0.0 89.8 jit_solution(726503232996676937)
XLA Ops:
  0.0 0.0 copy-start
  0.0 1.3 %copy.19 = bf16[2,256,4,128]{3,1,2,0:T(8,128)(2,1)S(1)} copy(bf16[2,256,4,128]{3,2,1,0:T(4,128)(2,1)} %param.4) | data formatting | bytes 1048576 | tf_op args[1]
  1.3 1.9 %collective-permute-start = (bf16[2,256,4,128]{3,1,2,0:T(8,128)(2,1)S(1)}, bf16[2,256,4,128]{3,1,2,0:T(8,128)(2,1)}, u32[]{:S(2)}, u32[]{:S(2)}) collective-permute-start(bf16[2,256,4,128]{3,1,2,0:T(8,128)(2,1)S(1)} %copy.19), channel_id=1, source_target_pairs={{0,2},{2,4},{4,6},{6,8},{8,10},{10,12},{12,14},{14,16},{16,18},{18... | collective-permute-start | bytes 1572872 | tf_op jit(solution)/shard_map/ppermute | solution.py:12
  3.3 1.0 %slice.27 = bf16[1,256,4,128]{3,2,1,0:T(4,128)(2,1)S(1)} slice(bf16[2,256,4,128]{3,2,1,0:T(4,128)(2,1)} %param.4), slice={[1:2], [0:256], [0:4], [0:128]} | slice | bytes 524288 | tf_op jit(solution)/shard_map/slice | solution.py:50
  4.3 0.8 reshape.334
  5.1 0.2 copy.53
  5.4 0.1 add_bitcast_fusion
  5.4 0.1 add_bitcast_fusion.2
  5.5 0.2 broadcast_compare_fusion
  5.7 0.0 copy-done
  5.7 2.1 %fusion.8 = (f32[4,8,256]{2,1,0:T(8,128)S(1)}, f32[4,256,256,8]{2,1,3,0:T(8,128)S(1)}) fusion(pred[256,256]{0,1:T(8,128)(4,1)S(1)} %get-tuple-element.25, bf16[256,4,8,128]{3,2,1,0:T(8,128)(2,1)S(1)} %bitcast.243, bf16[2,256,4,128]{3,1,2,0:T(8,128)(2,1)S(1)} %copy.19), kind=kOutput, calls=%fused_computation.16 | convolution fusion | flops 543154176 | bytes 10846208 | tf_op jit(solution)/shard_map/qghd,kgd->ghqk/dot_general | solution.py:39
  7.9 1.8 %fusion = f32[4,8,256]{2,1,0:T(8,128)S(1)} fusion(f32[4,256,256,8]{2,1,3,0:T(8,128)S(1)} %get-tuple-element.32, f32[4,8,256]{2,1,0:T(8,128)S(1)} %broadcast_maximum_fusion.3, pred[256,256]{0,1:T(8,128)(4,1)S(1)} %get-tuple-element.25), kind=kLoop, calls=%fused_computation.8 | loop fusion | flops 8380416 | bytes 8519680 | tf_op jit(solution)/shard_map/reduce_sum | solution.py:46
  9.7 2.2 %fusion.18 = f32[4,8,256,128]{2,3,1,0:T(8,128)S(1)} fusion(f32[4,256,256,8]{2,1,3,0:T(8,128)S(1)} %get-tuple-element.32, f32[4,8,256]{2,1,0:T(8,128)S(1)} %broadcast_maximum_fusion.3, pred[256,256]{0,1:T(8,128)(4,1)S(1)} %get-tuple-element.25, bf16[1,256,4,128]{1,3,2,0:T(8,128)(2,1)S(1)} %copy.53), kind=kOutput, calls=%fused_computation.23 | convolution fusion | flops 545259520 | bytes 12943360 | tf_op jit(solution)/shard_map/ghqk,kgd->ghqd/dot_general | solution.py:47
  11.9 10.2 %collective-permute-done = bf16[2,256,4,128]{3,1,2,0:T(8,128)(2,1)} collective-permute-done((bf16[2,256,4,128]{3,1,2,0:T(8,128)(2,1)S(1)}, bf16[2,256,4,128]{3,1,2,0:T(8,128)(2,1)}, u32[]{:S(2)}, u32[]{:S(2)}) %collective-permute-start) | collective-permute-done | bytes 524320 | tf_op jit(solution)/shard_map/ppermute | solution.py:12
  22.2 3.1 %fusion.9 = (f32[4,8,256]{2,1,0:T(8,128)S(1)}, f32[4,256,256,8]{2,1,3,0:T(8,128)S(1)}) fusion(pred[256,256]{0,1:T(8,128)(4,1)S(1)} %get-tuple-element.26, bf16[256,4,8,128]{3,2,1,0:T(8,128)(2,1)S(1)} %bitcast.246, bf16[2,256,4,128]{3,1,2,0:T(8,128)(2,1)} %collective-permute-done), kind=kOutput, calls=%fused_computation.17 | convolution fusion | flops 543154176 | bytes 10846208 | tf_op jit(solution)/shard_map/qghd,kgd->ghqk/dot_general | solution.py:39
  25.3 2.1 %collective-permute-start.1 = (bf16[2,256,4,128]{3,1,2,0:T(8,128)(2,1)}, bf16[2,256,4,128]{3,1,2,0:T(8,128)(2,1)S(1)}, u32[]{:S(2)}, u32[]{:S(2)}) collective-permute-start(bf16[2,256,4,128]{3,1,2,0:T(8,128)(2,1)} %collective-permute-done), channel_id=1, source_target_pairs={{0,2},{2,4},{4,6},{6,8},{8,10},{10,12},{12,14},{14,16},{16,18},{18... | collective-permute-start | bytes 1572872 | tf_op jit(solution)/shard_map/ppermute | solution.py:12
  27.4 3.0 %fusion.16 = f32[4,8,256,128]{2,3,1,0:T(8,128)S(1)} fusion(f32[4,256,256,8]{2,1,3,0:T(8,128)S(1)} %get-tuple-element.30, f32[4,8,256]{2,1,0:T(8,128)S(1)} %broadcast_maximum_fusion.2, pred[256,256]{0,1:T(8,128)(4,1)S(1)} %get-tuple-element.26, bf16[2,256,4,128]{3,1,2,0:T(8,128)(2,1)} %collective-permute-done), kind=kOutput, calls=%fused_computation.22 | convolution fusion | flops 545259520 | bytes 12943360 | tf_op jit(solution)/shard_map/ghqk,kgd->ghqd/dot_general | solution.py:47
  30.4 1.8 %fusion.2 = f32[4,8,256]{2,1,0:T(8,128)S(1)} fusion(f32[4,256,256,8]{2,1,3,0:T(8,128)S(1)} %get-tuple-element.30, f32[4,8,256]{2,1,0:T(8,128)S(1)} %broadcast_maximum_fusion.2, pred[256,256]{0,1:T(8,128)(4,1)S(1)} %get-tuple-element.26), kind=kLoop, calls=%fused_computation.10 | loop fusion | flops 8380416 | bytes 8519680 | tf_op jit(solution)/shard_map/reduce_sum | solution.py:46
  32.2 8.0 %collective-permute-done.1 = bf16[2,256,4,128]{3,1,2,0:T(8,128)(2,1)S(1)} collective-permute-done((bf16[2,256,4,128]{3,1,2,0:T(8,128)(2,1)}, bf16[2,256,4,128]{3,1,2,0:T(8,128)(2,1)S(1)}, u32[]{:S(2)}, u32[]{:S(2)}) %collective-permute-start.1) | collective-permute-done | bytes 524320 | tf_op jit(solution)/shard_map/ppermute | solution.py:12
  40.2 2.1 %fusion.10 = (f32[4,8,256]{2,1,0:T(8,128)S(1)}, f32[4,256,256,8]{2,1,3,0:T(8,128)S(1)}) fusion(pred[256,256]{0,1:T(8,128)(4,1)S(1)} %get-tuple-element.24, bf16[256,4,8,128]{3,2,1,0:T(8,128)(2,1)S(1)} %bitcast.245, bf16[2,256,4,128]{3,1,2,0:T(8,128)(2,1)S(1)} %collective-permute-done.1), kind=kOutput, calls=%fused_computation.18 | convolution fusion | flops 543154176 | bytes 10846208 | tf_op jit(solution)/shard_map/qghd,kgd->ghqk/dot_general | solution.py:39
  42.4 2.1 %collective-permute-start.2 = (bf16[2,256,4,128]{3,1,2,0:T(8,128)(2,1)S(1)}, bf16[2,256,4,128]{3,1,2,0:T(8,128)(2,1)S(1)}, u32[]{:S(2)}, u32[]{:S(2)}) collective-permute-start(bf16[2,256,4,128]{3,1,2,0:T(8,128)(2,1)S(1)} %collective-permute-done.1), channel_id=1, source_target_pairs={{0,2},{2,4},{4,6},{6,8},{8,10},{10,12},{12,14},{14,16},{16,18},{18... | collective-permute-start | bytes 1572872 | tf_op jit(solution)/shard_map/ppermute | solution.py:12
  44.5 2.0 %fusion.14 = f32[4,8,256,128]{2,3,1,0:T(8,128)S(1)} fusion(f32[4,256,256,8]{2,1,3,0:T(8,128)S(1)} %get-tuple-element.28, f32[4,8,256]{2,1,0:T(8,128)S(1)} %broadcast_maximum_fusion.1, pred[256,256]{0,1:T(8,128)(4,1)S(1)} %get-tuple-element.24, bf16[2,256,4,128]{3,1,2,0:T(8,128)(2,1)S(1)} %collective-permute-done.1), kind=kOutput, calls=%fused_computation.21 | convolution fusion | flops 545259520 | bytes 12943360 | tf_op jit(solution)/shard_map/ghqk,kgd->ghqd/dot_general | solution.py:47
  46.6 1.8 %fusion.4 = f32[4,8,256]{2,1,0:T(8,128)S(1)} fusion(f32[4,256,256,8]{2,1,3,0:T(8,128)S(1)} %get-tuple-element.28, f32[4,8,256]{2,1,0:T(8,128)S(1)} %broadcast_maximum_fusion.1, pred[256,256]{0,1:T(8,128)(4,1)S(1)} %get-tuple-element.24), kind=kLoop, calls=%fused_computation.12 | loop fusion | flops 8380416 | bytes 8519680 | tf_op jit(solution)/shard_map/reduce_sum | solution.py:46
  48.4 8.7 %collective-permute-done.2 = bf16[2,256,4,128]{3,1,2,0:T(8,128)(2,1)S(1)} collective-permute-done((bf16[2,256,4,128]{3,1,2,0:T(8,128)(2,1)S(1)}, bf16[2,256,4,128]{3,1,2,0:T(8,128)(2,1)S(1)}, u32[]{:S(2)}, u32[]{:S(2)}) %collective-permute-start.2) | collective-permute-done | bytes 524320 | tf_op jit(solution)/shard_map/ppermute | solution.py:12
  57.1 2.1 %fusion.11 = (f32[4,8,256]{2,1,0:T(8,128)S(1)}, f32[4,256,256,8]{2,1,3,0:T(8,128)S(1)}) fusion(pred[256,256]{0,1:T(8,128)(4,1)S(1)} %get-tuple-element.23, bf16[256,4,8,128]{3,2,1,0:T(8,128)(2,1)S(1)} %bitcast.244, bf16[2,256,4,128]{3,1,2,0:T(8,128)(2,1)S(1)} %collective-permute-done.2), kind=kOutput, calls=%fused_computation.19 | convolution fusion | flops 543154176 | bytes 10846208 | tf_op jit(solution)/shard_map/qghd,kgd->ghqk/dot_general | solution.py:39
  59.3 1.8 %fusion.6 = f32[4,8,256]{2,1,0:T(8,128)S(1)} fusion(f32[4,256,256,8]{2,1,3,0:T(8,128)S(1)} %get-tuple-element.34, f32[4,8,256]{2,1,0:T(8,128)S(1)} %broadcast_maximum_fusion, pred[256,256]{0,1:T(8,128)(4,1)S(1)} %get-tuple-element.23), kind=kLoop, calls=%fused_computation.14 | loop fusion | flops 8380416 | bytes 8519680 | tf_op jit(solution)/shard_map/reduce_sum | solution.py:46
  61.1 0.1 fusion.58
  61.1 5.0 %fusion.22 = bf16[256,4,8,128]{0,3,2,1:T(8,128)(2,1)} fusion(f32[4,8,256,128]{2,3,1,0:T(8,128)S(1)} %fusion.14, f32[4,8,256,128]{2,3,1,0:T(8,128)S(1)} %fusion.16, f32[4,8,256,128]{2,3,1,0:T(8,128)S(1)} %fusion.18, f32[256,4,8]{0,2,1:T(8,128)S(1)} %get-tuple-element.7, f32[256,4,8]{0,2,1:T(8,128)S(1)} %get-tuple-element.10, ...), kind=kOutput, calls=%fused_computation.27 | convolution fusion | flops 558891008 | bytes 23724032 | tf_op jit(solution)/shard_map/ghqk,kgd->ghqd/dot_general | solution.py:47
  66.2 1.7 %fusion.90 = (bf16[128,4,8,128]{0,3,2,1:T(8,128)(2,1)S(1)}, bf16[128,4,8,128]{0,3,2,1:T(8,128)(2,1)S(1)}) fusion(bf16[256,4,8,128]{0,3,2,1:T(8,128)(2,1)} %fusion.22), kind=kLoop, calls=%fused_computation.131 | loop fusion | bytes 4194304 | tf_op jit(solution)/shard_map/split | solution.py:79
  67.8 0.2 pad_maximum_fusion
  68.1 17.7 %all_to_all.5 = bf16[2,128,4096]{1,2,0:T(8,128)(2,1)} all-to-all(bf16[2,128,4096]{1,2,0:T(8,128)(2,1)S(1)} %pad_maximum_fusion), channel_id=1, replica_groups=mesh['ctx'=256,'kvh'=2] {'kvh'}, dimensions={0} | all-to-all | bytes 4194304 | tf_op jit(solution)/shard_map/all_to_all | solution.py:78
  85.7 4.1 %copy.52 = bf16[128,8192]{1,0:T(8,128)(2,1)} copy(bf16[128,8192]{0,1:T(8,128)(2,1)} %bitcast.247) | data formatting | bytes 4194304 | tf_op jit(solution)/shard_map/reshape | solution.py:77
  (6 shorter events, 0.1 us)
Async XLA Ops:
  0.0 5.7 %copy-start = (bf16[256,32,128]{2,1,0:T(8,128)(2,1)S(1)}, bf16[256,32,128]{2,1,0:T(8,128)(2,1)}, u32[]{:S(2)}) copy-start(bf16[256,32,128]{2,1,0:T(8,128)(2,1)} %param.3) | copy-start | bytes 6291460
  1.3 20.9 %collective-permute-start = (bf16[2,256,4,128]{3,1,2,0:T(8,128)(2,1)S(1)}, bf16[2,256,4,128]{3,1,2,0:T(8,128)(2,1)}, u32[]{:S(2)}, u32[]{:S(2)}) collective-permute-start(bf16[2,256,4,128]{3,1,2,0:T(8,128)(2,1)S(1)} %copy.19), channel_id=1, source_target_pairs={{0,2},{2,4},{4,6},{6,8},{8,10},{10,12},{12,14},{14,16},{16,18},{18... | collective-permute-start | bytes 1572872 | tf_op jit(solution)/shard_map/ppermute | solution.py:12
  25.3 14.9 %collective-permute-start.1 = (bf16[2,256,4,128]{3,1,2,0:T(8,128)(2,1)}, bf16[2,256,4,128]{3,1,2,0:T(8,128)(2,1)S(1)}, u32[]{:S(2)}, u32[]{:S(2)}) collective-permute-start(bf16[2,256,4,128]{3,1,2,0:T(8,128)(2,1)} %collective-permute-done), channel_id=1, source_target_pairs={{0,2},{2,4},{4,6},{6,8},{8,10},{10,12},{12,14},{14,16},{16,18},{18... | collective-permute-start | bytes 1572872 | tf_op jit(solution)/shard_map/ppermute | solution.py:12
  42.4 14.7 %collective-permute-start.2 = (bf16[2,256,4,128]{3,1,2,0:T(8,128)(2,1)S(1)}, bf16[2,256,4,128]{3,1,2,0:T(8,128)(2,1)S(1)}, u32[]{:S(2)}, u32[]{:S(2)}) collective-permute-start(bf16[2,256,4,128]{3,1,2,0:T(8,128)(2,1)S(1)} %collective-permute-done.1), channel_id=1, source_target_pairs={{0,2},{2,4},{4,6},{6,8},{8,10},{10,12},{12,14},{14,16},{16,18},{18... | collective-permute-start | bytes 1572872 | tf_op jit(solution)/shard_map/ppermute | solution.py:12
